TPU v7x, 128 devices: a whole 4x4x4 slice. The times are simulated.
128 devices in a mesh: seq: 32 (over x, z, core), mp: 4 (over y).
Axes of the slice: x: 4, y: 4, z: 4, core: 2. Of those that a mesh axis runs over, the one named last changes fastest.
Arguments:
- hidden: bfloat16 [16384, 4096], P('seq', 'mp'), may hold values from -6 to 6
- w_zx: bfloat16 [4096, 2, 4096], P(None, None, 'mp'), may hold values from -0.09375 to 0.09375
- w_bc: bfloat16 [4096, 2, 512], P(None, None, 'mp'), may hold values from -0.09375 to 0.09375
- w_dt: bfloat16 [4096, 64], P(None, 'mp'), may hold values from -0.09375 to 0.09375
- conv_x: float32 [4, 4096], P(None, 'mp'), may hold values from -3 to 3
- conv_x_bias: float32 [4096], P('mp'), may hold values from -3 to 3
- conv_bc: float32 [4, 2, 512], P(None, None, 'mp'), may hold values from -3 to 3
- conv_bc_bias: float32 [2, 512], P(None, 'mp'), may hold values from -3 to 3
- a_log: float32 [64], P('mp'), may hold values from -9.5 to -0.5
- dt_bias: float32 [64], P('mp'), may hold values from -4 to -1
- d_skip: float32 [64], P('mp'), may hold values from 0.5 to 4
- norm_gain: float32 [4096], P('mp'), may hold values from 0.4 to 1.6
- state_bank: float32 [2, 64, 64, 128], P(None, 'mp'), may hold values from -2 to 2
- conv_bank_x: bfloat16 [2, 3, 4096], P(None, None, 'mp'), may hold values from -5 to 5
- conv_bank_bc: bfloat16 [2, 3, 2, 512], P(None, None, None, 'mp'), may hold values from -5 to 5
- prompt_blocks: int32 [9], replicated, may hold values from 1 to 48, 64 in all
- prompt_order: int32 [9], replicated, may hold values from 0 to 8, each once
- resume_slot: int32 [9], replicated, may hold values from 0 to 2
Outputs:
- mixed: bfloat16 [16384, 4096], P('seq', 'mp')
Inputs may be any that keep to these rules, and one draw needn't show every extreme that they name: `prompt_blocks`: blocks of each prompt; they sum to 64 and the longest is exactly 48. `prompt_order`: A permutation of the prompts. `resume_slot`: 2 means a fresh start from zero state and zero convolution rows.
All inputs are finite; a program needn't handle non-finite values.
Results may differ from a plain program's by a relative error of at most 0.0068.
Values may be sent and summed in bfloat16 or wider, within the bound.
No kernel may reach another device: no remote copies, remote signals or barrier semaphores. Data moves between devices by JAX's collectives and lax.ppermute only.
A program may use at most 192 MiB of HBM per device.

v0:
```python
import jax
import jax.numpy as jnp
from jax import lax
from jax.sharding import PartitionSpec as P

WIDTH = 4096
HEAD_DIM = 64
STATE = 128
BLOCK = 256
KERNEL = 4
BANK = 2


def from_behind(value, axis, steps):
    count = lax.axis_size(axis)
    pairs = [(source, (source + steps) % count) for source in range(count)]
    return lax.ppermute(value, axis, pairs)


def combine(earlier, later):
    return (earlier[0] * later[0], later[0][:, None, None] * earlier[1] + later[1])


def per_device(
    hidden,
    w_zx,
    w_bc,
    w_dt,
    conv_x,
    conv_x_bias,
    conv_bc,
    conv_bc_bias,
    a_log,
    dt_bias,
    d_skip,
    norm_gain,
    state_bank,
    conv_bank_x,
    conv_bank_bc,
    prompt_blocks,
    prompt_order,
    resume_slot,
):
    devices = lax.axis_size("seq")
    place = lax.axis_index("seq")
    rows_dev = hidden.shape[0]
    blocks = rows_dev // BLOCK
    inner_dev = w_zx.shape[2]
    gstate_dev = w_bc.shape[2]
    heads_dev = w_dt.shape[1]
    groups_dev = gstate_dev // STATE
    per_group = heads_dev // groups_dev
    channels = inner_dev + 2 * gstate_dev
    prompts = prompt_blocks.shape[0]
    flat_zx = w_zx.reshape(WIDTH, 2 * inner_dev)
    flat_bc = w_bc.reshape(WIDTH, 2 * gstate_dev)
    piece = lax.all_gather(hidden, "mp", axis=1, tiled=True)
    zx_sum = jnp.dot(piece, flat_zx, preferred_element_type=jnp.float32)
    bc_sum = jnp.dot(piece, flat_bc, preferred_element_type=jnp.float32)
    dt_raw = jnp.dot(piece, w_dt, preferred_element_type=jnp.float32)
    zx = zx_sum.astype(jnp.bfloat16)
    bc = bc_sum.astype(jnp.bfloat16)
    gate = zx[:, :inner_dev]
    mixin = jnp.concatenate([zx[:, inner_dev:], bc], axis=1).reshape(blocks, BLOCK, channels)
    own_tails = mixin[:, BLOCK - (KERNEL - 1) :, :]
    arrived = from_behind(own_tails, "seq", 1)
    wrapped = jnp.concatenate([jnp.zeros_like(arrived[:1]), arrived[:-1]], axis=0)
    before = jnp.where(place > 0, arrived, wrapped)
    prompt_ids = jnp.arange(prompts, dtype=jnp.int32)
    order_hot = (prompt_order[:, None] == prompt_ids[None, :]).astype(jnp.int32)
    lengths = jnp.sum(order_hot * prompt_blocks[None, :], axis=1)
    slots = jnp.sum(order_hot * resume_slot[None, :], axis=1)
    ends = jnp.cumsum(lengths)
    starts = ends - lengths
    stream_ids = jnp.arange(blocks, dtype=jnp.int32) * devices + place
    inside = (
        (stream_ids[:, None] >= starts[None, :]) & (stream_ids[:, None] < ends[None, :])
    ).astype(jnp.int32)
    block_slot = jnp.sum(inside * slots[None, :], axis=1)
    first = jnp.any(stream_ids[:, None] == starts[None, :], axis=1)
    pick = (block_slot[:, None] == jnp.arange(BANK, dtype=jnp.int32)[None, :]).astype(jnp.float32)
    bank_state = jnp.einsum("cr,rhpn->chpn", pick, state_bank, precision=lax.Precision.HIGHEST)
    bank_rows = jnp.concatenate(
        [conv_bank_x, conv_bank_bc.reshape(BANK, KERNEL - 1, 2 * gstate_dev)], axis=2
    )
    bank_tail = jnp.einsum("cr,rkz->ckz", pick, bank_rows.astype(jnp.float32)).astype(jnp.bfloat16)
    tail = jnp.where(first[:, None, None], bank_tail, before)
    kernel = jnp.concatenate([conv_x, conv_bc.reshape(KERNEL, 2 * gstate_dev)], axis=1)
    bias = jnp.concatenate([conv_x_bias, conv_bc_bias.reshape(2 * gstate_dev)], axis=0)
    padded = jnp.concatenate([tail, mixin], axis=1).astype(jnp.float32)
    acc = bias[None, None, :] + padded[:, 0:BLOCK] * kernel[0]
    for k in range(1, KERNEL):
        acc = acc + padded[:, k : k + BLOCK] * kernel[k]
    conv = jax.nn.silu(acc).astype(jnp.bfloat16)
    xs = conv[..., :inner_dev].reshape(blocks, BLOCK, groups_dev, per_group, HEAD_DIM)
    bs = conv[..., inner_dev : inner_dev + gstate_dev].reshape(blocks, BLOCK, groups_dev, STATE)
    cq = conv[..., inner_dev + gstate_dev :].reshape(blocks, BLOCK, groups_dev, STATE)
    dt = jax.nn.softplus(dt_raw.reshape(blocks, BLOCK, heads_dev) + dt_bias[None, None, :])
    cum = jnp.cumsum(dt * (-jnp.exp(a_log))[None, None, :], axis=1)
    scores = jnp.einsum("cqgn,ckgn->cgqk", cq, bs, preferred_element_type=jnp.float32)
    cum_h = cum.transpose(0, 2, 1)
    lower = jnp.arange(BLOCK)[:, None] >= jnp.arange(BLOCK)[None, :]
    damp = jnp.exp(
        jnp.where(lower[None, None], cum_h[:, :, :, None] - cum_h[:, :, None, :], -jnp.inf)
    )
    damp = damp.reshape(blocks, groups_dev, per_group, BLOCK, BLOCK)
    dt_h = dt.transpose(0, 2, 1).reshape(blocks, groups_dev, per_group, 1, BLOCK)
    mix = (scores[:, :, None] * damp * dt_h).astype(jnp.bfloat16)
    y_intra = jnp.einsum("cgjqk,ckgjp->cqgjp", mix, xs, preferred_element_type=jnp.float32)
    last = cum[:, -1, :]
    grow = jnp.exp(last)
    factor = (dt * jnp.exp(last[:, None, :] - cum)).reshape(blocks, BLOCK, groups_dev, per_group, 1)
    weighted = (xs.astype(jnp.float32) * factor).astype(jnp.bfloat16)
    local_state = jnp.einsum(
        "cqgjp,cqgn->cgjpn", weighted, bs, preferred_element_type=jnp.float32
    ).reshape(blocks, heads_dev, HEAD_DIM, STATE)
    step_a = jnp.where(first[:, None], 0.0, grow)
    step_b = local_state + jnp.where(
        first[:, None, None, None], grow[:, :, None, None] * bank_state, 0.0
    )
    core = place % 2
    chip = place // 2
    chips = devices // 2
    half = heads_dev // 2
    rows = blocks * half

    def keep(part, at):
        piece = lax.dynamic_slice_in_dim(part, at * half, half, axis=1)
        return piece.reshape((rows,) + part.shape[2:])

    pair = [(source, source ^ 1) for source in range(devices)]
    mine = (keep(step_a, core), keep(step_b, core))
    got = lax.ppermute((keep(step_a, 1 - core), keep(step_b, 1 - core)), "seq", pair)
    early = jax.tree.map(lambda own, other: jnp.where(core == 0, own, other), mine, got)
    later = jax.tree.map(lambda own, other: jnp.where(core == 0, other, own), mine, got)
    quarter = half // 2
    split_heads = lambda part: [
        part.reshape((blocks, 2, quarter) + part.shape[1:])[:, g].reshape(
            (blocks * quarter,) + part.shape[1:]
        )
        for g in range(2)
    ]
    chip_a, chip_b = combine(early, later)
    lanes = [list(pair) for pair in zip(split_heads(chip_a), split_heads(chip_b))]
    priors = [[jnp.ones_like(lane[0]), jnp.zeros_like(lane[1])] for lane in lanes]

    def wrap(part, neutral, late):
        moved = jnp.concatenate(
            [jnp.full_like(part[:quarter], neutral), part[: part.shape[0] - quarter]], axis=0
        )
        return jnp.where(late, part, moved)

    span = 1
    while span < chips:
        late = chip >= span
        for g in range(2):
            got_a, got_b = from_behind(tuple(lanes[g]), "seq", 2 * span)
            lead = (wrap(got_a, 1.0, late), wrap(got_b, 0.0, late))
            lanes[g] = list(combine(lead, tuple(lanes[g])))
            priors[g] = list(combine(lead, tuple(priors[g])))
        span *= 2
    joined = []
    for g in range(2):
        run_a, run_b = lanes[g]
        prior_a, prior_b = priors[g]
        lift = combine((run_a[:quarter], run_b[:quarter]), (prior_a[quarter:], prior_b[quarter:]))[
            1
        ]
        joined.append(jnp.concatenate([prior_b[:quarter], lift], axis=0))
    before_chip = jnp.concatenate(
        [part.reshape((blocks, quarter) + part.shape[1:]) for part in joined], axis=1
    ).reshape(chip_b.shape)
    after_early = early[0][:, None, None] * before_chip + early[1]
    own_part = jnp.where(core == 0, before_chip, after_early)
    other_part = lax.ppermute(jnp.where(core == 0, after_early, before_chip), "seq", pair)
    split_rows = lambda part: part.reshape((blocks, half) + part.shape[1:])
    own_part, other_part = (split_rows(own_part), split_rows(other_part))
    previous = jnp.where(
        core == 0,
        jnp.concatenate([own_part, other_part], axis=1),
        jnp.concatenate([other_part, own_part], axis=1),
    )
    state_in = jnp.where(first[:, None, None, None], bank_state, previous)
    read = jnp.einsum(
        "cqgn,cgjpn->cqgjp",
        cq.astype(jnp.float32),
        state_in.reshape(blocks, groups_dev, per_group, HEAD_DIM, STATE),
        precision=lax.Precision.HIGHEST,
    )
    growth = jnp.exp(cum).reshape(blocks, BLOCK, groups_dev, per_group, 1)
    skip = d_skip.reshape(1, 1, groups_dev, per_group, 1)
    y_total = y_intra + growth * read + skip * xs.astype(jnp.float32)
    gated = y_total.reshape(rows_dev, inner_dev) * jax.nn.silu(gate.astype(jnp.float32))
    grouped = gated.reshape(rows_dev, groups_dev, inner_dev // groups_dev)
    scale = lax.rsqrt(jnp.mean(grouped * grouped, axis=2, keepdims=True) + 1e-05)
    result = (grouped * scale).reshape(rows_dev, inner_dev) * norm_gain[None, :]
    return result.astype(jnp.bfloat16)


def solution(mesh):
    placed = (
        P("seq", "mp"),
        P(None, None, "mp"),
        P(None, None, "mp"),
        P(None, "mp"),
        P(None, "mp"),
        P("mp"),
        P(None, None, "mp"),
        P(None, "mp"),
        P("mp"),
        P("mp"),
        P("mp"),
        P("mp"),
        P(None, "mp", None, None),
        P(None, None, "mp"),
        P(None, None, None, "mp"),
        P(),
        P(),
        P(),
    )
    return jax.shard_map(
        per_device, mesh=mesh, in_specs=placed, out_specs=P("seq", "mp"), check_vma=False
    )
```

profile of v0, /device:TPU:1, one launch (start us, length us, event | category | flops | bytes accessed | tf_op | source)
XLA Modules:
  0.0 195.6 jit_solution(3872452470648923946)
XLA Ops:
  6.5 0.7 all-gather.2.cloned.1.call-update
  7.3 0.9 select_reduce_fusion.1
  8.2 0.2 reduce-window.14
  8.4 17.2 %copy.111 = bf16[512,8,2,1024]{3,1,2,0:T(8,128)(2,1)} copy(bf16[512,8,2,1024]{3,2,1,0:T(2,128)(2,1)} %bitcast.142) | data formatting | bytes 33554432
  25.7 0.2 compare_reduce_fusion
  25.9 0.2 fusion.46
  26.2 34.1 %all-gather.2.cloned.1.call-done = bf16[512,4096]{1,0:T(8,128)(2,1)} async-done(((bf16[512,1024]{1,0:T(8,128)(2,1)}), bf16[512,4096]{1,0:T(8,128)(2,1)}) %all-gather.2.cloned.1.call-update) | async-done | bytes 4194320 | tf_op jit(solution)/shard_map/all_gather | solution.py:57
  60.3 15.8 %convolution_convert_fusion = bf16[512,2048]{1,0:T(8,128)(2,1)S(1)} fusion(bf16[512,4096]{1,0:T(8,128)(2,1)} %all-gather.2.cloned.1.call-done, bf16[4096,2048]{1,0:T(8,128)(2,1)} %bitcast.143), kind=kOutput, calls=%fused_computation.8 | convolution fusion | flops 8590983168 | bytes 23068672 | tf_op jit(solution)/shard_map/dot_general | solution.py:58
  76.2 2.2 %copy-done.16 = bf16[4096,2,128]{2,1,0:T(2,128)(2,1)S(1)} copy-done((bf16[4096,2,128]{2,1,0:T(2,128)(2,1)S(1)}, bf16[4096,2,128]{2,1,0:T(2,128)(2,1)}, u32[]{:S(2)}) %copy-start.16) | copy-done | bytes 2097176
  78.4 1.3 fusion.20
  79.9 2.1 %collective-permute-start = (bf16[2,3,1280]{2,0,1:T(2,128)(2,1)S(1)}, bf16[2,3,1280]{2,0,1:T(2,128)(2,1)S(1)}, u32[]{:S(2)}, u32[]{:S(2)}) collective-permute-start(bf16[2,3,1280]{2,0,1:T(2,128)(2,1)S(1)} %copy.107), channel_id=1, source_target_pairs={{0,4},{4,8},{8,12},{12,16},{16,20},{20,24},{24,28},{28,32},{32,36}... | collective-permute-start | bytes 46088 | tf_op jit(solution)/shard_map/ppermute | solution.py:17
  82.0 1.2 fusion.73
  83.1 0.1 copy_bitcast_fusion.1
  83.3 1.2 reduce-window.18
  84.4 0.2 slice_reduce_fusion
  84.7 0.2 slice_reduce_fusion.1
  84.9 0.1 fusion.62
  85.4 1.1 collective-permute-done.1
  86.7 1.3 collective-permute-start.2
  88.0 1.0 collective-permute-start.11
  89.0 0.2 broadcast_select_fusion
  89.2 0.3 maximum_convert_fusion
  89.5 1.7 multiply_convert_fusion.2
  91.2 1.4 slice_convert_fusion
  92.6 2.3 %copy.84 = bf16[2,256,1024]{1,2,0:T(8,128)(2,1)} copy(bf16[2,256,1024]{2,1,0:T(8,128)(2,1)} %get-tuple-element.33) | data formatting | bytes 2097152 | tf_op jit(solution)/shard_map/slice | solution.py:95
  94.9 1.7 fusion.23
  96.6 4.6 %copy_add_fusion = (f32[2,16,64,128]{3,0,2,1:T(2,128)S(1)}, f32[2,16,64,128]{3,0,2,1:T(2,128)}) fusion(f32[2,16,64,128]{3,2,1,0:T(8,128)S(1)} %fusion.23, pred[2]{0:T(512)(128)(4,1)S(1)} %compare_reduce_fusion, f32[2,16]{0,1:T(8,128)S(1)} %copy.89, f32[2,16,64,128]{3,2,1,0:T(8,128)S(1)} %copy-done, s32[2]{0:T(128)S(1)} %fusion.46), kind=kOutput, calls=%fused_computation.42 | convolution fusion | flops 7077892 | bytes 4194442 | tf_op jit(solution)/shard_map/cr,rhpn->chpn/dot_general | solution.py:82
  101.3 0.8 collective-permute-start.5
  102.2 2.5 %collective-permute-start.3 = (f32[8]{0:T(128)S(1)}, f32[8]{0:T(128)S(1)}, u32[]{:S(2)}, u32[]{:S(2)}) collective-permute-start(f32[8]{0:T(128)S(1)} %get-tuple-element.18), channel_id=1, source_target_pairs={{0,16},{4,20},{8,24},{12,28},{16,32},{20,36},{24,40},{28,44},{32,4... | collective-permute-start | bytes 104 | tf_op jit(solution)/shard_map/ppermute | solution.py:17
  104.8 1.4 collective-permute-start.12
  106.2 2.1 %collective-permute-done.3 = f32[8]{0:T(128)S(1)} collective-permute-done((f32[8]{0:T(128)S(1)}, f32[8]{0:T(128)S(1)}, u32[]{:S(2)}, u32[]{:S(2)}) %collective-permute-start.3) | collective-permute-done | bytes 64 | tf_op jit(solution)/shard_map/ppermute | solution.py:17
  108.4 0.1 fusion.31
  108.6 1.0 collective-permute-start.6
  109.6 1.3 collective-permute-done.12
  111.0 1.0 collective-permute-done.4
  112.0 1.6 collective-permute-start.10
  113.6 4.8 %collective-permute-done.6 = f32[8,64,128]{2,1,0:T(8,128)S(1)} collective-permute-done((f32[8,64,128]{2,1,0:T(8,128)S(1)}, f32[8,64,128]{2,1,0:T(8,128)S(1)}, u32[]{:S(2)}, u32[]{:S(2)}) %collective-permute-start.6) | collective-permute-done | bytes 262176 | tf_op jit(solution)/shard_map/ppermute | solution.py:17
  118.4 0.1 multiply_add_fusion.5
  118.7 1.2 collective-permute-start.18
  119.8 4.0 %collective-permute-done.14 = f32[8,64,128]{2,1,0:T(8,128)S(1)} collective-permute-done((f32[8,64,128]{2,1,0:T(8,128)S(1)}, f32[8,64,128]{2,1,0:T(8,128)S(1)}, u32[]{:S(2)}, u32[]{:S(2)}) %collective-permute-start.14) | collective-permute-done | bytes 262176 | tf_op jit(solution)/shard_map/ppermute | solution.py:17
  124.0 0.2 collective-permute-start.15
  124.2 4.8 %collective-permute-done.7 = f32[8,64,128]{2,1,0:T(8,128)S(1)} collective-permute-done((f32[8,64,128]{2,1,0:T(8,128)S(1)}, f32[8,64,128]{2,1,0:T(8,128)S(1)}, u32[]{:S(2)}, u32[]{:S(2)}) %collective-permute-start.7) | collective-permute-done | bytes 262176 | tf_op jit(solution)/shard_map/ppermute | solution.py:17
  129.3 5.3 %collective-permute-done.15 = f32[8,64,128]{2,1,0:T(8,128)S(1)} collective-permute-done((f32[8,64,128]{2,1,0:T(8,128)S(1)}, f32[8,64,128]{2,1,0:T(8,128)S(1)}, u32[]{:S(2)}, u32[]{:S(2)}) %collective-permute-start.15) | collective-permute-done | bytes 262176 | tf_op jit(solution)/shard_map/ppermute | solution.py:17
  134.8 0.8 collective-permute-done.8
  135.7 1.4 collective-permute-start.9
  137.3 5.9 %collective-permute-done.16 = f32[8,64,128]{2,1,0:T(8,128)S(1)} collective-permute-done((f32[8,64,128]{2,1,0:T(8,128)S(1)}, f32[8,64,128]{2,1,0:T(8,128)S(1)}, u32[]{:S(2)}, u32[]{:S(2)}) %collective-permute-start.16) | collective-permute-done | bytes 262176 | tf_op jit(solution)/shard_map/ppermute | solution.py:17
  143.4 0.3 collective-permute-start.17
  143.7 3.7 %collective-permute-done.9 = f32[8,64,128]{2,1,0:T(8,128)S(1)} collective-permute-done((f32[8,64,128]{2,1,0:T(8,128)S(1)}, f32[8,64,128]{2,1,0:T(8,128)S(1)}, u32[]{:S(2)}, u32[]{:S(2)}) %collective-permute-start.9) | collective-permute-done | bytes 262176 | tf_op jit(solution)/shard_map/ppermute | solution.py:17
  147.4 0.2 add_add_fusion.1
  147.7 5.8 %collective-permute-done.17 = f32[8,64,128]{2,1,0:T(8,128)S(1)} collective-permute-done((f32[8,64,128]{2,1,0:T(8,128)S(1)}, f32[8,64,128]{2,1,0:T(8,128)S(1)}, u32[]{:S(2)}, u32[]{:S(2)}) %collective-permute-start.17) | collective-permute-done | bytes 262176 | tf_op jit(solution)/shard_map/ppermute | solution.py:17
  153.6 0.2 add_add_fusion
  153.9 1.1 bitcast_select_fusion.1
  155.1 10.9 %collective-permute-start.19 = (f32[16,64,128]{2,1,0:T(8,128)}, f32[16,64,128]{2,1,0:T(8,128)}, u32[]{:S(2)}, u32[]{:S(2)}) collective-permute-start(f32[16,64,128]{2,1,0:T(8,128)} %get-tuple-element.31), channel_id=1, source_target_pairs={{0,4},{4,0},{8,12},{12,8},{16,20},{20,16},{24,28},{28,24},{32,36},... | collective-permute-start | bytes 1572872 | tf_op jit(solution)/shard_map/ppermute | solution.py:175
  166.0 1.8 copy.98
  167.9 1.3 fusion.37
  169.2 1.4 copy.93
  170.6 1.4 copy.94
  172.1 0.8 fusion.24
  173.0 2.1 %fusion.25 = f32[2,16,64,256]{3,2,1,0:T(8,128)S(1)} fusion(f32[2,16,64,128]{3,0,2,1:T(2,128)S(1)} %fusion.24, bf16[2,256,1280]{2,1,0:T(8,128)(2,1)} %copy-done.1), kind=kOutput, calls=%fused_computation.40 | convolution fusion | flops 805306368 | bytes 3276800 | tf_op jit(solution)/shard_map/cqgn,cgjpn->cqgjp/dot_general | solution.py:184
  175.0 2.6 %fusion.19 = f32[2,256,1,16,64]{1,4,3,0,2:T(8,128)S(1)} fusion(f32[2,16,64,256]{3,2,1,0:T(8,128)S(1)} %fusion.25, f32[2,256,1,16,64]{1,4,3,0,2:T(8,128)S(1)} %bitcast.149, bf16[2,256,16,64]{1,3,2,0:T(8,128)(2,1)S(1)} %bitcast.147, f32[2,16,256]{2,1,0:T(8,128)S(1)} %get-tuple-element.42, f32[2,16,256]{2,1,0:T(8,128)S(1)} %get-tuple-element.45, ...), kind=kOutput, calls=%fused_computation.30 | convolution fusion | flops 281018368 | bytes 8028224 | tf_op jit(solution)/shard_map/cgjqk,ckgjp->cqgjp/dot_general | solution.py:109
  177.7 3.8 %copy.105 = f32[2,256,1,16,64]{4,3,1,0,2:T(8,128)} copy(f32[2,256,1,16,64]{1,4,3,0,2:T(8,128)S(1)} %fusion.19) | data formatting | bytes 4194304 | tf_op jit(solution)/shard_map/reshape | solution.py:193
  181.5 3.5 %reshape.290 = f32[512,1024]{1,0:T(8,128)S(1)} reshape(f32[2,256,1,16,64]{4,3,1,0,2:T(8,128)} %copy.105) | data formatting | bytes 4194304 | tf_op jit(solution)/shard_map/reshape | solution.py:193
  185.0 2.1 %multiply_reduce_fusion = f32[512]{0:T(512)S(1)} fusion(f32[512,1024]{1,0:T(8,128)S(1)} %reshape.290, bf16[512,2048]{1,0:T(8,128)(2,1)} %copy-done.2), kind=kLoop, calls=%fused_computation.32 | loop fusion | flops 4193792 | bytes 3147776 | tf_op jit(solution)/shard_map/reduce_sum | solution.py:195
  187.1 1.7 multiply_convert_fusion.3
  (116 shorter events, 3.3 us)
Async XLA Ops:
  6.5 90.0 %copy-start = (f32[2,16,64,128]{3,2,1,0:T(8,128)S(1)}, f32[2,16,64,128]{3,2,1,0:T(8,128)}, u32[]{:S(2)}) copy-start(f32[2,16,64,128]{3,2,1,0:T(8,128)} %param.30) | copy-start | bytes 3145732
  6.5 53.7 %all-gather.2.cloned.1.call-start = ((), (), s32[]{:S(2)}) async-start(), calls=%async_computation | async-start | bytes 5242880 | tf_op jit(solution)/shard_map/all_gather | solution.py:57
  8.4 17.2 %copy-start.13 = (bf16[2,3,2,128]{3,2,1,0:T(2,128)(2,1)S(1)}, bf16[2,3,2,128]{3,2,1,0:T(2,128)(2,1)}, u32[]{:S(2)}) copy-start(bf16[2,3,2,128]{3,2,1,0:T(2,128)(2,1)} %param.32) | copy-start | bytes 9220
  8.4 17.3 %copy-start.11 = (f32[1024]{0:T(1024)S(1)}, f32[1024]{0:T(1024)}, u32[]{:S(2)}) copy-start(f32[1024]{0:T(1024)} %param.23) | copy-start | bytes 12292
  8.4 17.3 %copy-start.15 = (f32[2,128]{1,0:T(2,128)S(1)}, f32[2,128]{1,0:T(2,128)}, u32[]{:S(2)}) copy-start(f32[2,128]{1,0:T(2,128)} %param.25) | copy-start | bytes 3076
  8.4 17.3 %copy-start.9 = (f32[4,1024]{1,0:T(4,128)S(1)}, f32[4,1024]{1,0:T(4,128)}, u32[]{:S(2)}) copy-start(f32[4,1024]{1,0:T(4,128)} %param.22) | copy-start | bytes 49156
  8.4 17.7 %copy-start.12 = (f32[4,2,128]{2,1,0:T(2,128)S(1)}, f32[4,2,128]{2,1,0:T(2,128)}, u32[]{:S(2)}) copy-start(f32[4,2,128]{2,1,0:T(2,128)} %param.24) | copy-start | bytes 12292
  8.4 17.8 %copy-start.18 = (f32[16]{0:T(128)S(1)}, f32[16]{0:T(128)}, u32[]{:S(2)}) copy-start(f32[16]{0:T(128)} %param.26) | copy-start | bytes 196
  60.3 15.9 %copy-start.4 = (bf16[512,4096]{1,0:T(8,128)(2,1)S(1)}, bf16[512,4096]{1,0:T(8,128)(2,1)}, u32[]{:S(2)}) copy-start(bf16[512,4096]{1,0:T(8,128)(2,1)} %all-gather.2.cloned.1.call-done) | copy-start | bytes 12582916
  76.0 3.7 %copy-start.2 = (bf16[512,2048]{1,0:T(8,128)(2,1)}, bf16[512,2048]{1,0:T(8,128)(2,1)S(1)}, u32[]{:S(2)}) copy-start(bf16[512,2048]{1,0:T(8,128)(2,1)S(1)} %convolution_convert_fusion) | copy-start | bytes 6291460
  76.1 2.4 %copy-start.16 = (bf16[4096,2,128]{2,1,0:T(2,128)(2,1)S(1)}, bf16[4096,2,128]{2,1,0:T(2,128)(2,1)}, u32[]{:S(2)}) copy-start(bf16[4096,2,128]{2,1,0:T(2,128)(2,1)} %param.20) | copy-start | bytes 6291460
  79.7 2.2 %copy-start.8 = (bf16[4096,16]{0,1:T(8,128)(2,1)S(1)}, bf16[4096,16]{0,1:T(8,128)(2,1)}, u32[]{:S(2)}) copy-start(bf16[4096,16]{0,1:T(8,128)(2,1)} %param.21) | copy-start | bytes 393220
  79.9 3.3 %copy-start.14 = (f32[16]{0:T(128)S(1)}, f32[16]{0:T(128)}, u32[]{:S(2)}) copy-start(f32[16]{0:T(128)} %param.27) | copy-start | bytes 196
  79.9 9.1 %copy-start.17 = (bf16[2,3,1024]{2,0,1:T(2,128)(2,1)S(1)}, bf16[2,3,1024]{2,0,1:T(2,128)(2,1)}, u32[]{:S(2)}) copy-start(bf16[2,3,1024]{2,0,1:T(2,128)(2,1)} %param.31) | copy-start | bytes 36868
  79.9 9.1 %collective-permute-start = (bf16[2,3,1280]{2,0,1:T(2,128)(2,1)S(1)}, bf16[2,3,1280]{2,0,1:T(2,128)(2,1)S(1)}, u32[]{:S(2)}, u32[]{:S(2)}) collective-permute-start(bf16[2,3,1280]{2,0,1:T(2,128)(2,1)S(1)} %copy.107), channel_id=1, source_target_pairs={{0,4},{4,8},{8,12},{12,16},{16,20},{20,24},{24,28},{28,32},{32,36}... | collective-permute-start | bytes 46088 | tf_op jit(solution)/shard_map/ppermute | solution.py:17
  85.3 1.2 collective-permute-start.1
  86.7 15.5 %collective-permute-start.2 = (f32[8]{0:T(128)S(1)}, f32[8]{0:T(128)S(1)}, u32[]{:S(2)}, u32[]{:S(2)}) collective-permute-start(f32[8]{0:T(128)S(1)} %reshape_squeeze.12), channel_id=1, source_target_pairs={{0,8},{4,12},{8,16},{12,20},{16,24},{20,28},{24,32},{28,36},{32,40... | collective-permute-start | bytes 104 | tf_op jit(solution)/shard_map/ppermute | solution.py:17
  88.0 16.7 %collective-permute-start.11 = (f32[8]{0:T(128)S(1)}, f32[8]{0:T(128)S(1)}, u32[]{:S(2)}, u32[]{:S(2)}) collective-permute-start(f32[8]{0:T(128)S(1)} %reshape_squeeze.14), channel_id=1, source_target_pairs={{0,8},{4,12},{8,16},{12,20},{16,24},{20,28},{24,32},{28,36},{32,40... | collective-permute-start | bytes 104 | tf_op jit(solution)/shard_map/ppermute | solution.py:17
  91.2 1.4 copy-start.1
  101.3 7.1 %collective-permute-start.5 = (f32[16,64,128]{2,1,0:T(8,128)S(1)}, f32[16,64,128]{2,1,0:T(8,128)S(1)}, u32[]{:S(2)}, u32[]{:S(2)}) collective-permute-start(f32[16,64,128]{2,1,0:T(8,128)S(1)} %bitcast.155), channel_id=1, source_target_pairs={{0,4},{4,0},{8,12},{12,8},{16,20},{20,16},{24,28},{28,24},{32,36},... | collective-permute-start | bytes 1572872 | tf_op jit(solution)/shard_map/ppermute | solution.py:133
  102.2 6.0 %collective-permute-start.3 = (f32[8]{0:T(128)S(1)}, f32[8]{0:T(128)S(1)}, u32[]{:S(2)}, u32[]{:S(2)}) collective-permute-start(f32[8]{0:T(128)S(1)} %get-tuple-element.18), channel_id=1, source_target_pairs={{0,16},{4,20},{8,24},{12,28},{16,32},{20,36},{24,40},{28,44},{32,4... | collective-permute-start | bytes 104 | tf_op jit(solution)/shard_map/ppermute | solution.py:17
  104.8 6.0 %collective-permute-start.12 = (f32[8]{0:T(128)S(1)}, f32[8]{0:T(128)S(1)}, u32[]{:S(2)}, u32[]{:S(2)}) collective-permute-start(f32[8]{0:T(128)S(1)} %get-tuple-element.25), channel_id=1, source_target_pairs={{0,16},{4,20},{8,24},{12,28},{16,32},{20,36},{24,40},{28,44},{32,4... | collective-permute-start | bytes 104 | tf_op jit(solution)/shard_map/ppermute | solution.py:17
  108.3 3.6 %collective-permute-start.4 = (f32[8]{0:T(128)S(1)}, f32[8]{0:T(128)S(1)}, u32[]{:S(2)}, u32[]{:S(2)}) collective-permute-start(f32[8]{0:T(128)S(1)} %fusion.58), channel_id=1, source_target_pairs={{0,32},{4,36},{8,40},{12,44},{16,48},{20,52},{24,56},{28,60},{32,6... | collective-permute-start | bytes 104 | tf_op jit(solution)/shard_map/ppermute | solution.py:17
  108.6 9.8 %collective-permute-start.6 = (f32[8,64,128]{2,1,0:T(8,128)S(1)}, f32[8,64,128]{2,1,0:T(8,128)S(1)}, u32[]{:S(2)}, u32[]{:S(2)}) collective-permute-start(f32[8,64,128]{2,1,0:T(8,128)S(1)} %bitcast.154), channel_id=1, source_target_pairs={{0,8},{4,12},{8,16},{12,20},{16,24},{20,28},{24,32},{28,36},{32,40... | collective-permute-start | bytes 786440 | tf_op jit(solution)/shard_map/ppermute | solution.py:17
  110.9 7.7 %collective-permute-start.13 = (f32[8]{0:T(128)S(1)}, f32[8]{0:T(128)S(1)}, u32[]{:S(2)}, u32[]{:S(2)}) collective-permute-start(f32[8]{0:T(128)S(1)} %fusion.60), channel_id=1, source_target_pairs={{0,32},{4,36},{8,40},{12,44},{16,48},{20,52},{24,56},{28,60},{32,6... | collective-permute-start | bytes 104 | tf_op jit(solution)/shard_map/ppermute | solution.py:17
  112.0 17.1 %collective-permute-start.10 = (f32[8]{0:T(128)S(1)}, f32[8]{0:T(128)S(1)}, u32[]{:S(2)}, u32[]{:S(2)}) collective-permute-start(f32[8]{0:T(128)S(1)} %fusion.53), channel_id=1, source_target_pairs={{0,64},{4,68},{8,72},{12,76},{16,80},{20,84},{24,88},{28,92},{32,9... | collective-permute-start | bytes 104 | tf_op jit(solution)/shard_map/ppermute | solution.py:17
  113.6 10.3 %collective-permute-start.14 = (f32[8,64,128]{2,1,0:T(8,128)S(1)}, f32[8,64,128]{2,1,0:T(8,128)S(1)}, u32[]{:S(2)}, u32[]{:S(2)}) collective-permute-start(f32[8,64,128]{2,1,0:T(8,128)S(1)} %bitcast.153), channel_id=1, source_target_pairs={{0,8},{4,12},{8,16},{12,20},{16,24},{20,28},{24,32},{28,36},{32,40... | collective-permute-start | bytes 786440 | tf_op jit(solution)/shard_map/ppermute | solution.py:17
  118.5 10.5 %collective-permute-start.7 = (f32[8,64,128]{2,1,0:T(8,128)S(1)}, f32[8,64,128]{2,1,0:T(8,128)S(1)}, u32[]{:S(2)}, u32[]{:S(2)}) collective-permute-start(f32[8,64,128]{2,1,0:T(8,128)S(1)} %multiply_add_fusion.5), channel_id=1, source_target_pairs={{0,16},{4,20},{8,24},{12,28},{16,32},{20,36},{24,40},{28,44},{32,4... | collective-permute-start | bytes 786440 | tf_op jit(solution)/shard_map/ppermute | solution.py:17
  118.7 18.4 %collective-permute-start.18 = (f32[8]{0:T(128)S(1)}, f32[8]{0:T(128)S(1)}, u32[]{:S(2)}, u32[]{:S(2)}) collective-permute-start(f32[8]{0:T(128)S(1)} %fusion.55), channel_id=1, source_target_pairs={{0,64},{4,68},{8,72},{12,76},{16,80},{20,84},{24,88},{28,92},{32,9... | collective-permute-start | bytes 104 | tf_op jit(solution)/shard_map/ppermute | solution.py:17
  124.0 10.6 %collective-permute-start.15 = (f32[8,64,128]{2,1,0:T(8,128)S(1)}, f32[8,64,128]{2,1,0:T(8,128)S(1)}, u32[]{:S(2)}, u32[]{:S(2)}) collective-permute-start(f32[8,64,128]{2,1,0:T(8,128)S(1)} %multiply_add_fusion.2), channel_id=1, source_target_pairs={{0,16},{4,20},{8,24},{12,28},{16,32},{20,36},{24,40},{28,44},{32,4... | collective-permute-start | bytes 786440 | tf_op jit(solution)/shard_map/ppermute | solution.py:17
  129.1 6.5 %collective-permute-start.8 = (f32[8,64,128]{2,1,0:T(8,128)S(1)}, f32[8,64,128]{2,1,0:T(8,128)S(1)}, u32[]{:S(2)}, u32[]{:S(2)}) collective-permute-start(f32[8,64,128]{2,1,0:T(8,128)S(1)} %multiply_add_fusion.4), channel_id=1, source_target_pairs={{0,32},{4,36},{8,40},{12,44},{16,48},{20,52},{24,56},{28,60},{32,6... | collective-permute-start | bytes 786440 | tf_op jit(solution)/shard_map/ppermute | solution.py:17
  134.7 8.6 %collective-permute-start.16 = (f32[8,64,128]{2,1,0:T(8,128)S(1)}, f32[8,64,128]{2,1,0:T(8,128)S(1)}, u32[]{:S(2)}, u32[]{:S(2)}) collective-permute-start(f32[8,64,128]{2,1,0:T(8,128)S(1)} %multiply_add_fusion.1), channel_id=1, source_target_pairs={{0,32},{4,36},{8,40},{12,44},{16,48},{20,52},{24,56},{28,60},{32,6... | collective-permute-start | bytes 786440 | tf_op jit(solution)/shard_map/ppermute | solution.py:17
  135.7 11.7 %collective-permute-start.9 = (f32[8,64,128]{2,1,0:T(8,128)S(1)}, f32[8,64,128]{2,1,0:T(8,128)S(1)}, u32[]{:S(2)}, u32[]{:S(2)}) collective-permute-start(f32[8,64,128]{2,1,0:T(8,128)S(1)} %multiply_add_fusion.3), channel_id=1, source_target_pairs={{0,64},{4,68},{8,72},{12,76},{16,80},{20,84},{24,88},{28,92},{32,9... | collective-permute-start | bytes 786440 | tf_op jit(solution)/shard_map/ppermute | solution.py:17
  143.4 10.2 %collective-permute-start.17 = (f32[8,64,128]{2,1,0:T(8,128)S(1)}, f32[8,64,128]{2,1,0:T(8,128)S(1)}, u32[]{:S(2)}, u32[]{:S(2)}) collective-permute-start(f32[8,64,128]{2,1,0:T(8,128)S(1)} %multiply_add_fusion), channel_id=1, source_target_pairs={{0,64},{4,68},{8,72},{12,76},{16,80},{20,84},{24,88},{28,92},{32,9... | collective-permute-start | bytes 786440 | tf_op jit(solution)/shard_map/ppermute | solution.py:17
  155.1 15.5 %collective-permute-start.19 = (f32[16,64,128]{2,1,0:T(8,128)}, f32[16,64,128]{2,1,0:T(8,128)}, u32[]{:S(2)}, u32[]{:S(2)}) collective-permute-start(f32[16,64,128]{2,1,0:T(8,128)} %get-tuple-element.31), channel_id=1, source_target_pairs={{0,4},{4,0},{8,12},{12,8},{16,20},{20,16},{24,28},{28,24},{32,36},... | collective-permute-start | bytes 1572872 | tf_op jit(solution)/shard_map/ppermute | solution.py:175
  167.9 4.2 %copy-start.7 = (f32[2,16,64,128]{3,0,2,1:T(2,128)S(1)}, f32[2,16,64,128]{3,0,2,1:T(2,128)}, u32[]{:S(2)}) copy-start(f32[2,16,64,128]{3,0,2,1:T(2,128)} %get-tuple-element.52) | copy-start | bytes 3145732
  172.9 2.1 %copy-start.5 = (bf16[2,256,1024]{1,2,0:T(8,128)(2,1)S(1)}, bf16[2,256,1024]{1,2,0:T(8,128)(2,1)}, u32[]{:S(2)}) copy-start(bf16[2,256,1024]{1,2,0:T(8,128)(2,1)} %copy.84) | copy-start | bytes 3145732
  172.9 2.1 %copy-start.6 = (f32[2,256,1024]{1,2,0:T(8,128)S(1)}, f32[2,256,1024]{1,2,0:T(8,128)}, u32[]{:S(2)}) copy-start(f32[2,256,1024]{1,2,0:T(8,128)} %copy.98) | copy-start | bytes 6291460
  172.9 2.1 %copy-start.19 = (f32[16]{0:T(128)S(1)}, f32[16]{0:T(128)}, u32[]{:S(2)}) copy-start(f32[16]{0:T(128)} %param.28) | copy-start | bytes 196
  185.0 2.1 %copy-start.3 = (bf16[512,2048]{1,0:T(8,128)(2,1)S(1)}, bf16[512,2048]{1,0:T(8,128)(2,1)}, u32[]{:S(2)}) copy-start(bf16[512,2048]{1,0:T(8,128)(2,1)} %copy-done.2) | copy-start | bytes 6291460
  185.0 2.1 %copy-start.10 = (f32[1024]{0:T(1024)S(1)}, f32[1024]{0:T(1024)}, u32[]{:S(2)}) copy-start(f32[1024]{0:T(1024)} %param.29) | copy-start | bytes 12292
Sparse Core Ops, SparseCore 0:
  9.0 51.2 all-gather.1
where the time goes:
time: 196 us
  waiting for transfers between devices  75.5 us (39%)
  local copies, waits for them, and re-layouts  35.3 us (18%)
  matrix products  30.7 us (16%)
  starting transfers between devices  25.8 us (13%)
  other arithmetic  14.2 us (7%)
  between operations  14.1 us (7%)
    ppermute x17, waiting for transfers between devices, from_behind(): return lax.ppermute(value, axis, pairs)  39.6 us
    all_gather x1, waiting for transfers between devices, per_device(): piece = lax.all_gather(hidden, 'mp', axis=1, tiled=True)  34.1 us
    unnamed x44, local copies, waits for them, and re-layouts  19.5 us
    dot_general x1, matrix products, per_device(): zx_sum = jnp.dot(piece, flat_zx, preferred_element_type=jnp.float32)  15.8 us
    ppermute x17, starting transfers between devices, from_behind(): return lax.ppermute(value, axis, pairs)  14.1 us
    ppermute x1, starting transfers between devices, per_device(): lax.ppermute(jnp.where(core == 0, after_early, before_chip), 'seq', pair)  10.9 us
    reshape x2, local copies, waits for them, and re-layouts, per_device(): y_total.reshape(rows_dev, inner_dev) * jax.nn.silu(gate.astype(jnp.float32))  7.29 us
    dot_general x1, matrix products, per_device(): jnp.einsum('cr,rhpn->chpn', pick, state_bank, precision=lax.Precision.HIG...  4.63 us
  transfers between devices with their start and end apart: 21, of which 13 were waited for; matrix products, arithmetic and copies ran while one was open for 21% of the time, Pallas kernels for 0%

commit v1 on v0

--- a/solution.py
+++ b/solution.py
@@ -1,7 +1,9 @@
+import functools
 import jax
 import jax.numpy as jnp
 from jax import lax
 from jax.sharding import PartitionSpec as P
+from jax.lax import all_to_all, psum
 
 WIDTH = 4096
 HEAD_DIM = 64
@@ -9,6 +11,17 @@
 BLOCK = 256
 KERNEL = 4
 BANK = 2
+
+
+def squares_launch(x_local, k_dim):
+    p_count = psum(1, "mp")
+    line_up = [p_count if t == k_dim else 1 for t in range(x_local.ndim)]
+    fresh = jnp.tile(x_local, line_up)
+    tall = all_to_all(fresh, "mp", split_axis=k_dim, concat_axis=k_dim, tiled=True)
+    return tall
+
+
+matrix_shape = functools.partial(squares_launch, k_dim=1)
 
 
 def from_behind(value, axis, steps):
@@ -54,7 +67,7 @@
     prompts = prompt_blocks.shape[0]
     flat_zx = w_zx.reshape(WIDTH, 2 * inner_dev)
     flat_bc = w_bc.reshape(WIDTH, 2 * gstate_dev)
-    piece = lax.all_gather(hidden, "mp", axis=1, tiled=True)
+    piece = matrix_shape(hidden)
     zx_sum = jnp.dot(piece, flat_zx, preferred_element_type=jnp.float32)
     bc_sum = jnp.dot(piece, flat_bc, preferred_element_type=jnp.float32)
     dt_raw = jnp.dot(piece, w_dt, preferred_element_type=jnp.float32)

time: 196 us -> 214 us (1.092)
  local copies, waits for them, and re-layouts: 35.3 us -> 60.6 us
  between operations: 14.1 us -> 0.7 us
  starting transfers between devices: 25.8 us -> 29.1 us
  matrix products: 30.7 us -> 33 us
    all_gather x1 -> x0, waiting for transfers between devices: 34.1 us -> none  [per_device(): piece = lax.all_gather(hidden, 'mp', axis=1, tiled=True)]
    all_to_all x0 -> x1, waiting for transfers between devices: none -> 30.8 us  [squares_launch(): all_to_all(fresh, 'mp', split_axis=k_dim, concat_axis=k_dim, tiled=True)]
    all_to_all x0 -> x2, local copies, waits for them, and re-layouts: none -> 13.6 us  [squares_launch(): all_to_all(fresh, 'mp', split_axis=k_dim, concat_axis=k_dim, tiled=True)]
    dot_general x0 -> x1, local copies, waits for them, and re-layouts: none -> 7.85 us  [per_device(): dt_raw = jnp.dot(piece, w_dt, preferred_element_type=jnp.float32)]
    ppermute x17, waiting for transfers between devices: 39.6 us -> 45.1 us  [from_behind(): return lax.ppermute(value, axis, pairs)]
    all_to_all x0 -> x1, starting transfers between devices: none -> 5.13 us  [squares_launch(): all_to_all(fresh, 'mp', split_axis=k_dim, concat_axis=k_dim, tiled=True)]
    ppermute x17, starting transfers between devices: 14.1 us -> 9 us  [from_behind(): return lax.ppermute(value, axis, pairs)]
    ppermute x2, starting transfers between devices: 0.8 us -> 4.78 us  [per_device(): lax.ppermute((keep(step_a, 1 - core), keep(step_b, 1 - core)), 'seq', pair)]
  transfers between devices with their start and end apart: 21 -> 21, of which waited for: 13 -> 11; matrix products, arithmetic and copies ran while one was open for 21% -> 29% of each run, Pallas kernels for 0% -> 0%
where the time goes in v1:
time: 214 us; the launch traced here: 213 us
  waiting for transfers between devices  75.9 us (35%)
  local copies, waits for them, and re-layouts  60.6 us (28%)
  matrix products  33 us (15%)
  starting transfers between devices  29.1 us (14%)
  other arithmetic  13.5 us (6%)
    ppermute x17, waiting for transfers between devices, from_behind(): return lax.ppermute(value, axis, pairs)  45.1 us
    all_to_all x1, waiting for transfers between devices, squares_launch(): all_to_all(fresh, 'mp', split_axis=k_dim, concat_axis=k_dim, tiled=True)  30.8 us
    unnamed x50, local copies, waits for them, and re-layouts  19.5 us
    dot_general x1, matrix products, per_device(): zx_sum = jnp.dot(piece, flat_zx, preferred_element_type=jnp.float32)  15.8 us
    all_to_all x2, local copies, waits for them, and re-layouts, squares_launch(): all_to_all(fresh, 'mp', split_axis=k_dim, concat_axis=k_dim, tiled=True)  13.6 us
    ppermute x1, starting transfers between devices, per_device(): lax.ppermute(jnp.where(core == 0, after_early, before_chip), 'seq', pair)  10.2 us
    ppermute x17, starting transfers between devices, from_behind(): return lax.ppermute(value, axis, pairs)  9 us
    dot_general x1, local copies, waits for them, and re-layouts, per_device(): dt_raw = jnp.dot(piece, w_dt, preferred_element_type=jnp.float32)  7.85 us
  transfers between devices with their start and end apart: 21, of which 11 were waited for; matrix products, arithmetic and copies ran while one was open for 29% of the time, Pallas kernels for 0%

profile of v1, /device:TPU:1, one launch (start us, length us, event | category | flops | bytes accessed | tf_op | source)
XLA Modules:
  0.0 212.8 jit_solution(6849377573275255118)
XLA Ops:
  0.0 3.8 %tile.2 = bf16[512,4,1024]{2,0,1:T(8,128)(2,1)} broadcast(bf16[512,1024]{1,0:T(8,128)(2,1)} %param.18), dimensions={0,2} | broadcast | bytes 5242880 | tf_op jit(solution)/shard_map/tile | solution.py:19
  3.9 5.1 %all-to-all-start = ((bf16[512,4,1024]{2,0,1:T(8,128)(2,1)}), bf16[512,4,1024]{2,0,1:T(8,128)(2,1)}, u32[]{:S(2)}, u32[]{:S(2)}) async-start(bf16[512,4,1024]{2,0,1:T(8,128)(2,1)} %tile.2), calls=%async_computation | async-start | bytes 8388608 | tf_op jit(solution)/shard_map/all_to_all | solution.py:20
  9.0 0.2 select_reduce_fusion.1
  9.2 0.2 reduce-window.14
  9.4 17.1 %copy.127 = bf16[512,8,2,1024]{3,1,2,0:T(8,128)(2,1)} copy(bf16[512,8,2,1024]{3,2,1,0:T(2,128)(2,1)} %bitcast.148) | data formatting | bytes 33554432
  26.6 0.2 compare_reduce_fusion
  26.8 0.2 fusion.52
  27.1 30.8 %all-to-all-done = bf16[512,4,1024]{2,0,1:T(8,128)(2,1)} async-done(((bf16[512,4,1024]{2,0,1:T(8,128)(2,1)}), bf16[512,4,1024]{2,0,1:T(8,128)(2,1)}, u32[]{:S(2)}, u32[]{:S(2)}) %all-to-all-start) | async-done | bytes 4194336 | tf_op jit(solution)/shard_map/all_to_all | solution.py:20
  57.9 7.4 %copy.102 = bf16[512,4,1024]{2,1,0:T(4,128)(2,1)} copy(bf16[512,4,1024]{2,0,1:T(8,128)(2,1)} %all-to-all-done) | data formatting | bytes 8388608 | tf_op jit(solution)/shard_map/all_to_all | solution.py:20
  65.4 7.9 %dot_general.37 = bf16[2,256,4096]{2,1,0:T(8,128)(2,1)} reshape(bf16[512,4,1024]{2,1,0:T(4,128)(2,1)} %copy.102) | data formatting | bytes 8388608 | tf_op jit(solution)/shard_map/dot_general | solution.py:73
  73.2 3.4 %convolution_add_fusion = f32[2,256,16]{1,2,0:T(8,128)S(1)} fusion(bf16[2,256,4096]{2,1,0:T(8,128)(2,1)} %dot_general.37, bf16[4096,16]{0,1:T(8,128)(2,1)S(1)} %copy-done.8, f32[16]{0:T(128)S(1)} %copy-done.14), kind=kOutput, calls=%fused_computation.37 | convolution fusion | flops 67117056 | bytes 4358208 | tf_op jit(solution)/shard_map/dot_general | solution.py:73
  76.7 1.1 reduce-window.18
  77.8 0.2 slice_reduce_fusion
  78.1 0.2 slice_reduce_fusion.1
  78.3 0.1 bitcast_exponential_fusion
  78.6 1.6 collective-permute-start.1
  80.3 6.2 %copy.97 = bf16[512,4,1024]{0,2,1:T(8,128)(2,1)} copy(bf16[512,4,1024]{2,0,1:T(8,128)(2,1)} %all-to-all-done) | data formatting | bytes 8388608 | tf_op jit(solution)/shard_map/all_to_all | solution.py:20
  86.5 15.8 %convolution_convert_fusion = bf16[512,2048]{1,0:T(8,128)(2,1)S(1)} fusion(bf16[512,4096]{0,1:T(8,128)(2,1)} %bitcast.152, bf16[4096,2048]{1,0:T(8,128)(2,1)} %bitcast.149), kind=kOutput, calls=%fused_computation.8 | convolution fusion | flops 8590983168 | bytes 23068672 | tf_op jit(solution)/shard_map/dot_general | solution.py:71
  102.4 2.2 %copy-done.19 = bf16[4096,2,128]{2,1,0:T(2,128)(2,1)S(1)} copy-done((bf16[4096,2,128]{2,1,0:T(2,128)(2,1)S(1)}, bf16[4096,2,128]{2,1,0:T(2,128)(2,1)}, u32[]{:S(2)}) %copy-start.19) | copy-done | bytes 2097176
  104.7 1.3 fusion.20
  106.2 1.7 collective-permute-start
  108.1 1.6 collective-permute-start.2
  109.8 1.3 collective-permute-start.11
  111.2 0.2 broadcast_select_fusion
  111.4 0.3 maximum_convert_fusion
  111.7 1.7 multiply_convert_fusion.2
  113.5 1.4 slice_convert_fusion
  114.8 2.3 %copy.101 = bf16[2,256,1024]{1,2,0:T(8,128)(2,1)} copy(bf16[2,256,1024]{2,1,0:T(8,128)(2,1)} %get-tuple-element.33) | data formatting | bytes 2097152 | tf_op jit(solution)/shard_map/slice | solution.py:108
  117.1 1.7 fusion.23
  118.8 4.6 %copy_add_fusion = (f32[2,16,64,128]{3,0,2,1:T(2,128)S(1)}, f32[2,16,64,128]{3,0,2,1:T(2,128)}) fusion(f32[2,16,64,128]{3,2,1,0:T(8,128)S(1)} %fusion.23, pred[2]{0:T(512)(128)(4,1)S(1)} %compare_reduce_fusion, f32[2,16]{0,1:T(8,128)S(1)} %copy.106, f32[2,16,64,128]{3,2,1,0:T(8,128)S(1)} %copy-done, s32[2]{0:T(128)S(1)} %fusion.52), kind=kOutput, calls=%fused_computation.43 | convolution fusion | flops 7077892 | bytes 4194442 | tf_op jit(solution)/shard_map/cr,rhpn->chpn/dot_general | solution.py:95
  123.5 3.2 %collective-permute-start.5 = (f32[16,64,128]{2,1,0:T(8,128)S(1)}, f32[16,64,128]{2,1,0:T(8,128)S(1)}, u32[]{:S(2)}, u32[]{:S(2)}) collective-permute-start(f32[16,64,128]{2,1,0:T(8,128)S(1)} %bitcast.163), channel_id=1, source_target_pairs={{0,4},{4,0},{8,12},{12,8},{16,20},{20,16},{24,28},{28,24},{32,36},... | collective-permute-start | bytes 1572872 | tf_op jit(solution)/shard_map/ppermute | solution.py:146
  126.9 1.7 collective-permute-start.12
  128.6 4.3 %collective-permute-done.3 = f32[8]{0:T(128)S(1)} collective-permute-done((f32[8]{0:T(128)S(1)}, f32[8]{0:T(128)S(1)}, u32[]{:S(2)}, u32[]{:S(2)}) %collective-permute-start.3) | collective-permute-done | bytes 64 | tf_op jit(solution)/shard_map/ppermute | solution.py:30
  133.0 0.1 fusion.31
  133.4 3.2 %collective-permute-done.4 = f32[8]{0:T(128)S(1)} collective-permute-done((f32[8]{0:T(128)S(1)}, f32[8]{0:T(128)S(1)}, u32[]{:S(2)}, u32[]{:S(2)}) %collective-permute-start.4) | collective-permute-done | bytes 64 | tf_op jit(solution)/shard_map/ppermute | solution.py:30
  136.6 0.7 collective-permute-start.10
  137.3 6.0 %collective-permute-done.6 = f32[8,64,128]{2,1,0:T(8,128)S(1)} collective-permute-done((f32[8,64,128]{2,1,0:T(8,128)S(1)}, f32[8,64,128]{2,1,0:T(8,128)S(1)}, u32[]{:S(2)}, u32[]{:S(2)}) %collective-permute-start.6) | collective-permute-done | bytes 262176 | tf_op jit(solution)/shard_map/ppermute | solution.py:30
  143.2 0.1 multiply_add_fusion.5
  143.6 5.4 %collective-permute-done.14 = f32[8,64,128]{2,1,0:T(8,128)S(1)} collective-permute-done((f32[8,64,128]{2,1,0:T(8,128)S(1)}, f32[8,64,128]{2,1,0:T(8,128)S(1)}, u32[]{:S(2)}, u32[]{:S(2)}) %collective-permute-start.14) | collective-permute-done | bytes 262176 | tf_op jit(solution)/shard_map/ppermute | solution.py:30
  148.9 0.1 multiply_add_fusion.2
  149.1 4.3 %collective-permute-done.7 = f32[8,64,128]{2,1,0:T(8,128)S(1)} collective-permute-done((f32[8,64,128]{2,1,0:T(8,128)S(1)}, f32[8,64,128]{2,1,0:T(8,128)S(1)}, u32[]{:S(2)}, u32[]{:S(2)}) %collective-permute-start.7) | collective-permute-done | bytes 262176 | tf_op jit(solution)/shard_map/ppermute | solution.py:30
  153.7 5.4 %collective-permute-done.15 = f32[8,64,128]{2,1,0:T(8,128)S(1)} collective-permute-done((f32[8,64,128]{2,1,0:T(8,128)S(1)}, f32[8,64,128]{2,1,0:T(8,128)S(1)}, u32[]{:S(2)}, u32[]{:S(2)}) %collective-permute-start.15) | collective-permute-done | bytes 262176 | tf_op jit(solution)/shard_map/ppermute | solution.py:30
  159.2 0.1 multiply_add_fusion.1
  159.3 0.7 collective-permute-done.8
  160.1 0.1 multiply_add_fusion.3
  160.2 1.5 collective-permute-start.9
  161.9 6.4 %collective-permute-done.16 = f32[8,64,128]{2,1,0:T(8,128)S(1)} collective-permute-done((f32[8,64,128]{2,1,0:T(8,128)S(1)}, f32[8,64,128]{2,1,0:T(8,128)S(1)}, u32[]{:S(2)}, u32[]{:S(2)}) %collective-permute-start.16) | collective-permute-done | bytes 262176 | tf_op jit(solution)/shard_map/ppermute | solution.py:30
  168.5 3.5 %collective-permute-done.9 = f32[8,64,128]{2,1,0:T(8,128)S(1)} collective-permute-done((f32[8,64,128]{2,1,0:T(8,128)S(1)}, f32[8,64,128]{2,1,0:T(8,128)S(1)}, u32[]{:S(2)}, u32[]{:S(2)}) %collective-permute-start.9) | collective-permute-done | bytes 262176 | tf_op jit(solution)/shard_map/ppermute | solution.py:30
  172.0 0.2 add_add_fusion.1
  172.3 6.0 %collective-permute-done.17 = f32[8,64,128]{2,1,0:T(8,128)S(1)} collective-permute-done((f32[8,64,128]{2,1,0:T(8,128)S(1)}, f32[8,64,128]{2,1,0:T(8,128)S(1)}, u32[]{:S(2)}, u32[]{:S(2)}) %collective-permute-start.17) | collective-permute-done | bytes 262176 | tf_op jit(solution)/shard_map/ppermute | solution.py:30
  178.3 0.2 add_add_fusion
  178.7 1.2 bitcast_select_fusion.1
  179.8 10.2 %collective-permute-start.19 = (f32[16,64,128]{2,1,0:T(8,128)}, f32[16,64,128]{2,1,0:T(8,128)}, u32[]{:S(2)}, u32[]{:S(2)}) collective-permute-start(f32[16,64,128]{2,1,0:T(8,128)} %get-tuple-element.31), channel_id=1, source_target_pairs={{0,4},{4,0},{8,12},{12,8},{16,20},{20,16},{24,28},{28,24},{32,36},... | collective-permute-start | bytes 1572872 | tf_op jit(solution)/shard_map/ppermute | solution.py:188
  190.0 1.8 copy.115
  191.9 1.3 fusion.38
  193.2 1.4 copy.110
  194.6 1.4 copy.111
  196.1 0.8 fusion.24
  197.0 2.1 fusion.25
  199.1 2.6 %fusion.19 = f32[2,256,1,16,64]{1,4,3,0,2:T(8,128)S(1)} fusion(f32[2,16,64,256]{3,2,1,0:T(8,128)S(1)} %fusion.25, f32[2,256,1,16,64]{1,4,3,0,2:T(8,128)S(1)} %bitcast.157, bf16[2,256,16,64]{1,3,2,0:T(8,128)(2,1)S(1)} %bitcast.155, f32[2,16,256]{2,1,0:T(8,128)S(1)} %get-tuple-element.46, f32[2,16,256]{2,1,0:T(8,128)S(1)} %get-tuple-element.44, ...), kind=kOutput, calls=%fused_computation.30 | convolution fusion | flops 281018368 | bytes 8028224 | tf_op jit(solution)/shard_map/cgjqk,ckgjp->cqgjp/dot_general | solution.py:122
  201.7 3.8 %copy.122 = f32[2,256,1,16,64]{4,3,1,0,2:T(8,128)} copy(f32[2,256,1,16,64]{1,4,3,0,2:T(8,128)S(1)} %fusion.19) | data formatting | bytes 4194304 | tf_op jit(solution)/shard_map/reshape | solution.py:206
  205.5 3.5 %reshape.297 = f32[512,1024]{1,0:T(8,128)S(1)} reshape(f32[2,256,1,16,64]{4,3,1,0,2:T(8,128)} %copy.122) | data formatting | bytes 4194304 | tf_op jit(solution)/shard_map/reshape | solution.py:206
  209.0 2.1 multiply_reduce_fusion
  211.1 1.7 multiply_convert_fusion.3
  (126 shorter events, 3.4 us)
Async XLA Ops:
  0.0 118.8 %copy-start = (f32[2,16,64,128]{3,2,1,0:T(8,128)S(1)}, f32[2,16,64,128]{3,2,1,0:T(8,128)}, u32[]{:S(2)}) copy-start(f32[2,16,64,128]{3,2,1,0:T(8,128)} %param.30) | copy-start | bytes 3145732
  3.8 5.1 %copy-start.16 = (s32[9]{0:T(128)S(1)}, s32[9]{0:T(128)}, u32[]{:S(2)}) copy-start(s32[9]{0:T(128)} %param.33) | copy-start | bytes 112
  3.8 5.1 %copy-start.17 = (s32[9]{0:T(128)S(1)}, s32[9]{0:T(128)}, u32[]{:S(2)}) copy-start(s32[9]{0:T(128)} %param.34) | copy-start | bytes 112
  3.9 5.1 %copy-start.18 = (s32[9]{0:T(128)S(1)}, s32[9]{0:T(128)}, u32[]{:S(2)}) copy-start(s32[9]{0:T(128)} %param.35) | copy-start | bytes 112
  3.9 54.1 %all-to-all-start = ((bf16[512,4,1024]{2,0,1:T(8,128)(2,1)}), bf16[512,4,1024]{2,0,1:T(8,128)(2,1)}, u32[]{:S(2)}, u32[]{:S(2)}) async-start(bf16[512,4,1024]{2,0,1:T(8,128)(2,1)} %tile.2), calls=%async_computation | async-start | bytes 8388608 | tf_op jit(solution)/shard_map/all_to_all | solution.py:20
  9.4 17.2 %copy-start.13 = (bf16[2,3,2,128]{3,2,1,0:T(2,128)(2,1)S(1)}, bf16[2,3,2,128]{3,2,1,0:T(2,128)(2,1)}, u32[]{:S(2)}) copy-start(bf16[2,3,2,128]{3,2,1,0:T(2,128)(2,1)} %param.32) | copy-start | bytes 9220
  9.4 17.2 %copy-start.11 = (f32[1024]{0:T(1024)S(1)}, f32[1024]{0:T(1024)}, u32[]{:S(2)}) copy-start(f32[1024]{0:T(1024)} %param.23) | copy-start | bytes 12292
  9.4 17.2 %copy-start.15 = (f32[2,128]{1,0:T(2,128)S(1)}, f32[2,128]{1,0:T(2,128)}, u32[]{:S(2)}) copy-start(f32[2,128]{1,0:T(2,128)} %param.25) | copy-start | bytes 3076
  9.4 17.2 %copy-start.9 = (f32[4,1024]{1,0:T(4,128)S(1)}, f32[4,1024]{1,0:T(4,128)}, u32[]{:S(2)}) copy-start(f32[4,1024]{1,0:T(4,128)} %param.22) | copy-start | bytes 49156
  9.4 17.6 %copy-start.12 = (f32[4,2,128]{2,1,0:T(2,128)S(1)}, f32[4,2,128]{2,1,0:T(2,128)}, u32[]{:S(2)}) copy-start(f32[4,2,128]{2,1,0:T(2,128)} %param.24) | copy-start | bytes 12292
  9.4 17.7 %copy-start.21 = (f32[16]{0:T(128)S(1)}, f32[16]{0:T(128)}, u32[]{:S(2)}) copy-start(f32[16]{0:T(128)} %param.26) | copy-start | bytes 196
  65.3 7.9 %copy-start.8 = (bf16[4096,16]{0,1:T(8,128)(2,1)S(1)}, bf16[4096,16]{0,1:T(8,128)(2,1)}, u32[]{:S(2)}) copy-start(bf16[4096,16]{0,1:T(8,128)(2,1)} %param.21) | copy-start | bytes 393220
  65.4 7.9 %copy-start.14 = (f32[16]{0:T(128)S(1)}, f32[16]{0:T(128)}, u32[]{:S(2)}) copy-start(f32[16]{0:T(128)} %param.27) | copy-start | bytes 196
  78.6 29.3 %collective-permute-start.1 = (f32[16]{0:T(128)S(1)}, f32[16]{0:T(128)S(1)}, u32[]{:S(2)}, u32[]{:S(2)}) collective-permute-start(f32[16]{0:T(128)S(1)} %reshape.280), channel_id=1, source_target_pairs={{0,4},{4,0},{8,12},{12,8},{16,20},{20,16},{24,28},{28,24},{32,36},... | collective-permute-start | bytes 200 | tf_op jit(solution)/shard_map/ppermute | solution.py:146
  86.5 15.9 %copy-start.4 = (bf16[512,4,1024]{0,2,1:T(8,128)(2,1)S(1)}, bf16[512,4,1024]{0,2,1:T(8,128)(2,1)}, u32[]{:S(2)}) copy-start(bf16[512,4,1024]{0,2,1:T(8,128)(2,1)} %copy.97) | copy-start | bytes 12582916
  102.3 3.7 %copy-start.2 = (bf16[512,2048]{1,0:T(8,128)(2,1)}, bf16[512,2048]{1,0:T(8,128)(2,1)S(1)}, u32[]{:S(2)}) copy-start(bf16[512,2048]{1,0:T(8,128)(2,1)S(1)} %convolution_convert_fusion) | copy-start | bytes 6291460
  102.3 2.4 %copy-start.19 = (bf16[4096,2,128]{2,1,0:T(2,128)(2,1)S(1)}, bf16[4096,2,128]{2,1,0:T(2,128)(2,1)}, u32[]{:S(2)}) copy-start(bf16[4096,2,128]{2,1,0:T(2,128)(2,1)} %param.20) | copy-start | bytes 6291460
  106.0 5.2 %copy-start.20 = (bf16[2,3,1024]{2,0,1:T(2,128)(2,1)S(1)}, bf16[2,3,1024]{2,0,1:T(2,128)(2,1)}, u32[]{:S(2)}) copy-start(bf16[2,3,1024]{2,0,1:T(2,128)(2,1)} %param.31) | copy-start | bytes 36868
  106.2 5.0 %collective-permute-start = (bf16[2,3,1280]{2,0,1:T(2,128)(2,1)S(1)}, bf16[2,3,1280]{2,0,1:T(2,128)(2,1)S(1)}, u32[]{:S(2)}, u32[]{:S(2)}) collective-permute-start(bf16[2,3,1280]{2,0,1:T(2,128)(2,1)S(1)} %copy.124), channel_id=1, source_target_pairs={{0,4},{4,8},{8,12},{12,16},{16,20},{20,24},{24,28},{28,32},{32,36}... | collective-permute-start | bytes 46088 | tf_op jit(solution)/shard_map/ppermute | solution.py:30
  108.1 18.6 %collective-permute-start.2 = (f32[8]{0:T(128)S(1)}, f32[8]{0:T(128)S(1)}, u32[]{:S(2)}, u32[]{:S(2)}) collective-permute-start(f32[8]{0:T(128)S(1)} %reshape_squeeze.12), channel_id=1, source_target_pairs={{0,8},{4,12},{8,16},{12,20},{16,24},{20,28},{24,32},{28,36},{32,40... | collective-permute-start | bytes 104 | tf_op jit(solution)/shard_map/ppermute | solution.py:30
  109.8 17.0 %collective-permute-start.11 = (f32[8]{0:T(128)S(1)}, f32[8]{0:T(128)S(1)}, u32[]{:S(2)}, u32[]{:S(2)}) collective-permute-start(f32[8]{0:T(128)S(1)} %reshape_squeeze.14), channel_id=1, source_target_pairs={{0,8},{4,12},{8,16},{12,20},{16,24},{20,28},{24,32},{28,36},{32,40... | collective-permute-start | bytes 104 | tf_op jit(solution)/shard_map/ppermute | solution.py:30
  113.4 1.4 copy-start.1
  123.5 9.4 %collective-permute-start.5 = (f32[16,64,128]{2,1,0:T(8,128)S(1)}, f32[16,64,128]{2,1,0:T(8,128)S(1)}, u32[]{:S(2)}, u32[]{:S(2)}) collective-permute-start(f32[16,64,128]{2,1,0:T(8,128)S(1)} %bitcast.163), channel_id=1, source_target_pairs={{0,4},{4,0},{8,12},{12,8},{16,20},{20,16},{24,28},{28,24},{32,36},... | collective-permute-start | bytes 1572872 | tf_op jit(solution)/shard_map/ppermute | solution.py:146
  126.8 6.0 %collective-permute-start.3 = (f32[8]{0:T(128)S(1)}, f32[8]{0:T(128)S(1)}, u32[]{:S(2)}, u32[]{:S(2)}) collective-permute-start(f32[8]{0:T(128)S(1)} %get-tuple-element.18), channel_id=1, source_target_pairs={{0,16},{4,20},{8,24},{12,28},{16,32},{20,36},{24,40},{28,44},{32,4... | collective-permute-start | bytes 104 | tf_op jit(solution)/shard_map/ppermute | solution.py:30
  126.9 6.4 %collective-permute-start.12 = (f32[8]{0:T(128)S(1)}, f32[8]{0:T(128)S(1)}, u32[]{:S(2)}, u32[]{:S(2)}) collective-permute-start(f32[8]{0:T(128)S(1)} %get-tuple-element.25), channel_id=1, source_target_pairs={{0,16},{4,20},{8,24},{12,28},{16,32},{20,36},{24,40},{28,44},{32,4... | collective-permute-start | bytes 104 | tf_op jit(solution)/shard_map/ppermute | solution.py:30
  132.9 3.6 %collective-permute-start.4 = (f32[8]{0:T(128)S(1)}, f32[8]{0:T(128)S(1)}, u32[]{:S(2)}, u32[]{:S(2)}) collective-permute-start(f32[8]{0:T(128)S(1)} %fusion.64), channel_id=1, source_target_pairs={{0,32},{4,36},{8,40},{12,44},{16,48},{20,52},{24,56},{28,60},{32,6... | collective-permute-start | bytes 104 | tf_op jit(solution)/shard_map/ppermute | solution.py:30
  133.2 10.1 %collective-permute-start.6 = (f32[8,64,128]{2,1,0:T(8,128)S(1)}, f32[8,64,128]{2,1,0:T(8,128)S(1)}, u32[]{:S(2)}, u32[]{:S(2)}) collective-permute-start(f32[8,64,128]{2,1,0:T(8,128)S(1)} %bitcast.162), channel_id=1, source_target_pairs={{0,8},{4,12},{8,16},{12,20},{16,24},{20,28},{24,32},{28,36},{32,40... | collective-permute-start | bytes 786440 | tf_op jit(solution)/shard_map/ppermute | solution.py:30
  133.3 10.1 %collective-permute-start.13 = (f32[8]{0:T(128)S(1)}, f32[8]{0:T(128)S(1)}, u32[]{:S(2)}, u32[]{:S(2)}) collective-permute-start(f32[8]{0:T(128)S(1)} %fusion.66), channel_id=1, source_target_pairs={{0,32},{4,36},{8,40},{12,44},{16,48},{20,52},{24,56},{28,60},{32,6... | collective-permute-start | bytes 104 | tf_op jit(solution)/shard_map/ppermute | solution.py:30
  136.6 17.0 %collective-permute-start.10 = (f32[8]{0:T(128)S(1)}, f32[8]{0:T(128)S(1)}, u32[]{:S(2)}, u32[]{:S(2)}) collective-permute-start(f32[8]{0:T(128)S(1)} %fusion.59), channel_id=1, source_target_pairs={{0,64},{4,68},{8,72},{12,76},{16,80},{20,84},{24,88},{28,92},{32,9... | collective-permute-start | bytes 104 | tf_op jit(solution)/shard_map/ppermute | solution.py:30
  137.3 11.7 %collective-permute-start.14 = (f32[8,64,128]{2,1,0:T(8,128)S(1)}, f32[8,64,128]{2,1,0:T(8,128)S(1)}, u32[]{:S(2)}, u32[]{:S(2)}) collective-permute-start(f32[8,64,128]{2,1,0:T(8,128)S(1)} %bitcast.161), channel_id=1, source_target_pairs={{0,8},{4,12},{8,16},{12,20},{16,24},{20,28},{24,32},{28,36},{32,40... | collective-permute-start | bytes 786440 | tf_op jit(solution)/shard_map/ppermute | solution.py:30
  143.3 10.1 %collective-permute-start.7 = (f32[8,64,128]{2,1,0:T(8,128)S(1)}, f32[8,64,128]{2,1,0:T(8,128)S(1)}, u32[]{:S(2)}, u32[]{:S(2)}) collective-permute-start(f32[8,64,128]{2,1,0:T(8,128)S(1)} %multiply_add_fusion.5), channel_id=1, source_target_pairs={{0,16},{4,20},{8,24},{12,28},{16,32},{20,36},{24,40},{28,44},{32,4... | collective-permute-start | bytes 786440 | tf_op jit(solution)/shard_map/ppermute | solution.py:30
  143.5 18.1 %collective-permute-start.18 = (f32[8]{0:T(128)S(1)}, f32[8]{0:T(128)S(1)}, u32[]{:S(2)}, u32[]{:S(2)}) collective-permute-start(f32[8]{0:T(128)S(1)} %fusion.61), channel_id=1, source_target_pairs={{0,64},{4,68},{8,72},{12,76},{16,80},{20,84},{24,88},{28,92},{32,9... | collective-permute-start | bytes 104 | tf_op jit(solution)/shard_map/ppermute | solution.py:30
  149.0 10.1 %collective-permute-start.15 = (f32[8,64,128]{2,1,0:T(8,128)S(1)}, f32[8,64,128]{2,1,0:T(8,128)S(1)}, u32[]{:S(2)}, u32[]{:S(2)}) collective-permute-start(f32[8,64,128]{2,1,0:T(8,128)S(1)} %multiply_add_fusion.2), channel_id=1, source_target_pairs={{0,16},{4,20},{8,24},{12,28},{16,32},{20,36},{24,40},{28,44},{32,4... | collective-permute-start | bytes 786440 | tf_op jit(solution)/shard_map/ppermute | solution.py:30
  153.5 6.5 %collective-permute-start.8 = (f32[8,64,128]{2,1,0:T(8,128)S(1)}, f32[8,64,128]{2,1,0:T(8,128)S(1)}, u32[]{:S(2)}, u32[]{:S(2)}) collective-permute-start(f32[8,64,128]{2,1,0:T(8,128)S(1)} %multiply_add_fusion.4), channel_id=1, source_target_pairs={{0,32},{4,36},{8,40},{12,44},{16,48},{20,52},{24,56},{28,60},{32,6... | collective-permute-start | bytes 786440 | tf_op jit(solution)/shard_map/ppermute | solution.py:30
  159.3 9.0 %collective-permute-start.16 = (f32[8,64,128]{2,1,0:T(8,128)S(1)}, f32[8,64,128]{2,1,0:T(8,128)S(1)}, u32[]{:S(2)}, u32[]{:S(2)}) collective-permute-start(f32[8,64,128]{2,1,0:T(8,128)S(1)} %multiply_add_fusion.1), channel_id=1, source_target_pairs={{0,32},{4,36},{8,40},{12,44},{16,48},{20,52},{24,56},{28,60},{32,6... | collective-permute-start | bytes 786440 | tf_op jit(solution)/shard_map/ppermute | solution.py:30
  160.2 11.8 %collective-permute-start.9 = (f32[8,64,128]{2,1,0:T(8,128)S(1)}, f32[8,64,128]{2,1,0:T(8,128)S(1)}, u32[]{:S(2)}, u32[]{:S(2)}) collective-permute-start(f32[8,64,128]{2,1,0:T(8,128)S(1)} %multiply_add_fusion.3), channel_id=1, source_target_pairs={{0,64},{4,68},{8,72},{12,76},{16,80},{20,84},{24,88},{28,92},{32,9... | collective-permute-start | bytes 786440 | tf_op jit(solution)/shard_map/ppermute | solution.py:30
  168.4 9.9 %collective-permute-start.17 = (f32[8,64,128]{2,1,0:T(8,128)S(1)}, f32[8,64,128]{2,1,0:T(8,128)S(1)}, u32[]{:S(2)}, u32[]{:S(2)}) collective-permute-start(f32[8,64,128]{2,1,0:T(8,128)S(1)} %multiply_add_fusion), channel_id=1, source_target_pairs={{0,64},{4,68},{8,72},{12,76},{16,80},{20,84},{24,88},{28,92},{32,9... | collective-permute-start | bytes 786440 | tf_op jit(solution)/shard_map/ppermute | solution.py:30
  179.8 14.8 %collective-permute-start.19 = (f32[16,64,128]{2,1,0:T(8,128)}, f32[16,64,128]{2,1,0:T(8,128)}, u32[]{:S(2)}, u32[]{:S(2)}) collective-permute-start(f32[16,64,128]{2,1,0:T(8,128)} %get-tuple-element.31), channel_id=1, source_target_pairs={{0,4},{4,0},{8,12},{12,8},{16,20},{20,16},{24,28},{28,24},{32,36},... | collective-permute-start | bytes 1572872 | tf_op jit(solution)/shard_map/ppermute | solution.py:188
  191.9 4.2 %copy-start.7 = (f32[2,16,64,128]{3,0,2,1:T(2,128)S(1)}, f32[2,16,64,128]{3,0,2,1:T(2,128)}, u32[]{:S(2)}) copy-start(f32[2,16,64,128]{3,0,2,1:T(2,128)} %get-tuple-element.53) | copy-start | bytes 3145732
  196.9 2.1 copy-start.5
  197.0 2.1 copy-start.6
  197.0 2.1 copy-start.22
  209.0 2.1 copy-start.3
  209.0 2.1 copy-start.10
